TPU v7x, 512 devices: a whole 4x8x8 slice. The times are simulated.
512 devices in a mesh: dp: 32 (over z, y_lo, core), feat: 16 (over y_hi, x).
Axes of the slice: x: 4, y: 8 (y_hi: 4, y_lo: 2; y = y_hi * 2 + y_lo), z: 8, core: 2. Of those that a mesh axis runs over, the one named last changes fastest.
Arguments:
- tokens: bfloat16 [8192, 8192], P('dp', 'feat'), may hold values from -6 to 6
- up_left: bfloat16 [16, 512, 2048], P('feat', 'dp'), may hold values from -0.25 to 0.25
- up_right: bfloat16 [2048, 16, 16], P('feat'), may hold values from -1.5 to 1.5
- down_left: bfloat16 [16, 2048, 512], P('feat', 'dp'), may hold values from -0.125 to 0.125
- down_right: bfloat16 [512, 16, 16], P('feat'), may hold values from -1.5 to 1.5
- layer_grad: bfloat16 [8192, 8192], P('dp', 'feat'), may hold values from -6 to 6
Outputs:
- layer_out: bfloat16 [8192, 8192], P('dp', 'feat')
- grad_tokens: bfloat16 [8192, 8192], P('dp', 'feat')
- grad_up_left: float32 [16, 512, 2048], P('feat', 'dp')
- grad_up_right: float32 [2048, 16, 16], P('feat')
- grad_down_left: float32 [16, 2048, 512], P('feat', 'dp')
- grad_down_right: float32 [512, 16, 16], P('feat')
All inputs are finite; a program needn't handle non-finite values.
Results may differ from a plain program's by a relative error of at most 0.0067.
Values may be sent and summed in bfloat16 or wider, within the bound.
No kernel may reach another device: no remote copies, remote signals or barrier semaphores. Data moves between devices by JAX's collectives and lax.ppermute only.
A program may use at most 128 MiB of HBM per device.

v0:
```python
import jax
import jax.numpy as jnp
import numpy as np
from jax import lax
from jax.sharding import Mesh
from jax.sharding import PartitionSpec as P

TILE_UP = 128
TILE_DOWN = 32
DP_AXES = ("z", "ylo", "core")
FEAT_AXES = ("yhi", "x")


def split_mesh(mesh):
    n_dp = mesh.shape["dp"]
    n_feat = mesh.shape["feat"]
    sizes = (n_dp // 4, 2, 2, n_feat // 4, 4)
    devices = np.asarray(mesh.devices).reshape(sizes)
    return Mesh(devices, DP_AXES + FEAT_AXES)


def exchange(wired):
    rows, feat_count, piece = wired.shape
    n_x = lax.axis_size("x")
    n_y = feat_count // n_x
    shaped = wired.reshape(rows, n_y, n_x, piece)
    shaped = lax.all_to_all(shaped, "x", 2, 2, tiled=True)
    shaped = lax.all_to_all(shaped, "yhi", 1, 1, tiled=True)
    return shaped.reshape(rows, feat_count, piece)


def dp_reduce_scatter(part, row_axis):
    shape = part.shape
    rows = shape[row_axis]
    n_z = lax.axis_size("z")
    split = shape[:row_axis] + (n_z, 2, 2, rows // (4 * n_z)) + shape[row_axis + 1 :]
    x = part.reshape(split)
    x = lax.psum_scatter(x, "core", scatter_dimension=row_axis + 2, tiled=True)
    x = lax.psum_scatter(x, "z", scatter_dimension=row_axis, tiled=True)
    x = lax.psum_scatter(x, "ylo", scatter_dimension=row_axis + 1, tiled=True)
    return x.reshape(shape[:row_axis] + (rows // (4 * n_z),) + shape[row_axis + 1 :])


def dp_all_gather(local, row_axis):
    shape = local.shape
    rows = shape[row_axis]
    x = local.reshape(shape[:row_axis] + (1, 1, 1, rows) + shape[row_axis + 1 :])
    x = lax.all_gather(x, "ylo", axis=row_axis + 1, tiled=True)
    x = lax.all_gather(x, "z", axis=row_axis, tiled=True)
    x = lax.all_gather(x, "core", axis=row_axis + 2, tiled=True)
    total = x.shape[row_axis] * x.shape[row_axis + 1] * x.shape[row_axis + 2] * rows
    return x.reshape(shape[:row_axis] + (total,) + shape[row_axis + 1 :])


def to_wire(blocks, feat_count):
    tok_rows, local_blocks, full_width = blocks.shape
    piece = full_width // feat_count
    shaped = blocks.reshape(tok_rows, local_blocks, feat_count, piece).transpose(0, 2, 1, 3)
    return shaped.reshape(tok_rows, feat_count, local_blocks * piece)


def from_wire(wired, local_blocks):
    tok_rows, feat_count, line_len = wired.shape
    piece = line_len // local_blocks
    shaped = wired.reshape(tok_rows, feat_count, local_blocks, piece).transpose(0, 2, 1, 3)
    return shaped.reshape(tok_rows, local_blocks, feat_count * piece)


def on_device(tokens, up_left, up_right, down_left, down_right, layer_grad):
    tok_rows = tokens.shape[0]
    local_blocks = up_left.shape[0]
    hidden_width = up_left.shape[2]
    block_width = down_left.shape[2]
    blocks_all = up_right.shape[1]
    group_up = up_right.shape[0]
    group_down = down_right.shape[0]
    feat_count = lax.axis_size("yhi") * lax.axis_size("x")
    n_dp = lax.axis_size("z") * lax.axis_size("ylo") * lax.axis_size("core")
    grad_scale = float(tok_rows * n_dp) ** (-0.5)
    tiles_up = group_up // TILE_UP
    tiles_down = group_down // TILE_DOWN
    up_full = dp_all_gather(up_left, 1)
    token_blocks = tokens.reshape(tok_rows, local_blocks, block_width)
    up_inner = jnp.einsum(
        "tbi,big->tbg", token_blocks, up_full, preferred_element_type=jnp.float32
    ).astype(jnp.bfloat16)
    up_mixed = exchange(to_wire(up_inner, feat_count))
    preact = jnp.einsum("tjg,gjk->tkg", up_mixed, up_right, preferred_element_type=jnp.float32)
    sigmoid_val = jax.nn.sigmoid(preact)
    activated = (
        (preact * sigmoid_val)
        .reshape(tok_rows, blocks_all, tiles_up, TILE_UP)
        .transpose(0, 2, 1, 3)
    )
    hidden = activated.reshape(tok_rows, local_blocks, hidden_width).astype(jnp.bfloat16)
    down_full = dp_all_gather(down_left, 1)
    down_inner = jnp.einsum(
        "tbh,bhc->tbc", hidden, down_full, preferred_element_type=jnp.float32
    ).astype(jnp.bfloat16)
    down_mixed = exchange(to_wire(down_inner, feat_count)).reshape(
        tok_rows, blocks_all * group_down
    )
    identity = jnp.eye(group_down, dtype=jnp.bfloat16).reshape(group_down, tiles_down, TILE_DOWN)
    mix_matrix = jnp.einsum(
        "cjk,cal->jcakl", down_right, identity, preferred_element_type=jnp.float32
    )
    mix_matrix = mix_matrix.astype(jnp.bfloat16).reshape(
        blocks_all * group_down, blocks_all * group_down
    )
    layer_out = jnp.dot(down_mixed, mix_matrix, preferred_element_type=jnp.float32).astype(
        jnp.bfloat16
    )
    grad_down_mixed = lax.dot_general(
        layer_grad, mix_matrix, (((1,), (1,)), ((), ())), preferred_element_type=jnp.float32
    ).astype(jnp.bfloat16)
    grad_by_group = layer_grad.reshape(tok_rows, tiles_down, blocks_all, TILE_DOWN).transpose(
        0, 2, 1, 3
    )
    grad_by_group = grad_by_group.reshape(tok_rows, blocks_all, group_down)
    right_down_term = (
        jnp.einsum(
            "tjc,tkc->cjk",
            down_mixed.reshape(tok_rows, blocks_all, group_down),
            grad_by_group,
            preferred_element_type=jnp.float32,
        )
        * grad_scale
    )
    grad_down_inner = from_wire(
        exchange(grad_down_mixed.reshape(tok_rows, feat_count, local_blocks * group_down)),
        local_blocks,
    )
    grad_down_left = dp_reduce_scatter(
        jnp.einsum("tbh,tbc->hbc", hidden, grad_down_inner, preferred_element_type=jnp.float32)
        * grad_scale,
        0,
    ).transpose(1, 0, 2)
    grad_hidden = jnp.einsum(
        "tbc,bhc->tbh", grad_down_inner, down_full, preferred_element_type=jnp.float32
    )
    grad_hidden = grad_hidden.reshape(tok_rows, tiles_up, blocks_all, TILE_UP).transpose(0, 2, 1, 3)
    grad_hidden = grad_hidden.reshape(tok_rows, blocks_all, group_up)
    grad_preact = (grad_hidden * sigmoid_val * (1.0 + preact * (1.0 - sigmoid_val))).astype(
        jnp.bfloat16
    )
    grad_up_mixed = jnp.einsum(
        "tkg,gjk->tjg", grad_preact, up_right, preferred_element_type=jnp.float32
    ).astype(jnp.bfloat16)
    right_up_term = (
        jnp.einsum("tjg,tkg->gjk", up_mixed, grad_preact, preferred_element_type=jnp.float32)
        * grad_scale
    )
    grad_up_inner = from_wire(exchange(grad_up_mixed), local_blocks)
    grad_tokens = jnp.einsum(
        "tbg,big->tbi", grad_up_inner, up_full, preferred_element_type=jnp.float32
    ).astype(jnp.bfloat16)
    grad_tokens = grad_tokens.reshape(tok_rows, local_blocks * block_width)
    grad_up_left = dp_reduce_scatter(
        jnp.einsum("tbi,tbg->ibg", token_blocks, grad_up_inner, preferred_element_type=jnp.float32)
        * grad_scale,
        0,
    ).transpose(1, 0, 2)
    rights = jnp.concatenate([right_up_term, right_down_term], axis=0)
    rights = lax.psum(rights, DP_AXES)
    grad_up_right = rights[:group_up]
    grad_down_right = rights[group_up:]
    return (layer_out, grad_tokens, grad_up_left, grad_up_right, grad_down_left, grad_down_right)


def solution(mesh):
    fine = split_mesh(mesh)
    row = P(DP_AXES, FEAT_AXES)
    weight = P(FEAT_AXES, DP_AXES, None)
    mixer = P(FEAT_AXES, None, None)
    return jax.shard_map(
        on_device,
        mesh=fine,
        in_specs=(row, weight, mixer, weight, mixer, row),
        out_specs=(row, row, weight, mixer, weight, mixer),
        check_vma=False,
    )
```

profile of v0, /device:TPU:1, one launch (start us, length us, event | category | flops | bytes accessed | tf_op | source)
XLA Modules:
  0.0 650.3 jit_solution(2913419054008153790)
XLA Ops:
  7.2 6.3 all-gather
  13.6 42.4 %all-gather.13.cloned.1.call-done = bf16[16,16,2048]{2,1,0:T(8,128)(2,1)} async-done(((bf16[2,16,2048]{2,1,0:T(8,128)(2,1)}), bf16[16,16,2048]{2,1,0:T(8,128)(2,1)}) %all-gather.13.cloned.1.call-update) | async-done | bytes 1048592 | tf_op jit(solution)/shard_map/all_gather | solution.py:49
  56.1 5.3 all-gather.2
  70.8 10.1 %all-gather.9.cloned.1.call-done = bf16[1,8,2,2,16,2048]{5,4,3,2,1,0:T(8,128)(2,1)} async-done(((bf16[1,8,2,1,16,2048]{5,4,3,2,1,0:T(8,128)(2,1)}), bf16[1,8,2,2,16,2048]{5,4,3,2,1,0:T(8,128)(2,1)}) %all-gather.9.cloned.1.call-update) | async-done | bytes 2097168 | tf_op jit(solution)/shard_map/all_gather | solution.py:50
  87.9 32.6 %all-gather.15.cloned.1.call-done = bf16[16,64,512]{2,1,0:T(8,128)(2,1)} async-done(((bf16[2,64,512]{2,1,0:T(8,128)(2,1)}), bf16[16,64,512]{2,1,0:T(8,128)(2,1)}) %all-gather.15.cloned.1.call-update) | async-done | bytes 1048592 | tf_op jit(solution)/shard_map/all_gather | solution.py:49
  121.3 6.5 all-to-all-start.5
  128.8 6.9 %all-to-all-done.5 = bf16[256,4,4,32]{0,3,2,1:T(8,128)(2,1)S(1)} async-done(((bf16[256,4,4,32]{0,3,2,1:T(8,128)(2,1)}), bf16[256,4,4,32]{0,3,2,1:T(8,128)(2,1)S(1)}, u32[]{:S(2)}, u32[]{:S(2)}) %all-to-all-start.5) | async-done | bytes 262176 | tf_op jit(solution)/shard_map/all_to_all | solution.py:28
  135.7 4.3 all-to-all-start.1
  141.2 4.1 all-gather.11.cloned.1.call-done
  147.6 18.1 %all-to-all-done.1 = bf16[256,4,4,128]{0,3,2,1:T(8,128)(2,1)} async-done(((bf16[256,4,4,128]{0,3,2,1:T(8,128)(2,1)}), bf16[256,4,4,128]{0,3,2,1:T(8,128)(2,1)}, u32[]{:S(2)}, u32[]{:S(2)}) %all-to-all-start.1) | async-done | bytes 1048608 | tf_op jit(solution)/shard_map/all_to_all | solution.py:28
  165.8 4.5 fusion.7
  172.3 15.0 %all_to_all.40 = bf16[256,4,4,128]{0,3,1,2:T(8,128)(2,1)S(1)} all-to-all(bf16[256,4,4,128]{0,3,1,2:T(8,128)(2,1)S(1)} %copy.95), channel_id=1, replica_groups=mesh['z'=8,'ylo'=2,'core'=2,'yhi'=4,'x'=4] {'x'}, dimensions={2} | all-to-all | bytes 2097152 | tf_op jit(solution)/shard_map/all_to_all | solution.py:27
  188.4 6.5 %all-to-all-start.7 = ((bf16[256,4,4,128]{0,3,2,1:T(8,128)(2,1)}), bf16[256,4,4,128]{0,3,2,1:T(8,128)(2,1)S(1)}, u32[]{:S(2)}, u32[]{:S(2)}) async-start(bf16[256,4,4,128]{0,3,2,1:T(8,128)(2,1)} %copy.96), calls=%async_computation.7 | async-start | bytes 2097152 | tf_op jit(solution)/shard_map/all_to_all | solution.py:28
  199.0 5.4 copy.103
  204.5 10.2 %all-to-all-done.7 = bf16[256,4,4,128]{0,3,2,1:T(8,128)(2,1)S(1)} async-done(((bf16[256,4,4,128]{0,3,2,1:T(8,128)(2,1)}), bf16[256,4,4,128]{0,3,2,1:T(8,128)(2,1)S(1)}, u32[]{:S(2)}, u32[]{:S(2)}) %all-to-all-start.7) | async-done | bytes 1048608 | tf_op jit(solution)/shard_map/all_to_all | solution.py:28
  218.7 53.0 %all-reduce.8.cloned.1.call-done = (f32[8,2,2,16,1,2048]{5,3,4,2,1,0:T(8,128)}, f32[8,2,2,64,1,512]{5,3,2,1,0,4:T(8,128)}) async-done(((f32[8,2,2,16,1,2048]{5,3,4,2,1,0:T(8,128)}, f32[8,2,2,64,1,512]{5,3,2,1,0,4:T(8,128)}), (f32[8,2,2,16,1,2048]{5,3,4,2,1,0:T(8,128)}, f32[8,2,2,64,1,512]{5,3,2,1,0,4:T(8,128)})) %all-reduce.8.cloned.1.call-update) | async-done | bytes 8388624
  283.2 9.2 %all_to_all.41 = bf16[256,4,4,32]{0,3,1,2:T(8,128)(2,1)S(1)} all-to-all(bf16[256,4,4,32]{0,3,1,2:T(8,128)(2,1)S(1)} %copy.87), channel_id=1, replica_groups=mesh['z'=8,'ylo'=2,'core'=2,'yhi'=4,'x'=4] {'x'}, dimensions={2} | all-to-all | bytes 524288 | tf_op jit(solution)/shard_map/all_to_all | solution.py:27
  293.1 6.5 all-to-all-start.3
  302.9 5.1 all-to-all-done.3
  309.3 7.6 %reduce-scatter.13.cloned.1.call-done = f32[1,2,1,64,1,512]{5,3,2,1,0,4:T(8,128)} async-done(((f32[8,2,1,64,1,512]{5,3,2,1,0,4:T(8,128)}), f32[1,2,1,64,1,512]{5,3,2,1,0,4:T(8,128)}) %reduce-scatter.13.cloned.1.call-update) | async-done | bytes 262160 | tf_op jit(solution)/shard_map/reduce_scatter | solution.py:39
  317.0 46.2 %reduce-scatter.9.cloned.1.call-done = f32[1,2,1,16,1,2048]{5,3,4,2,1,0:T(8,128)} async-done(((f32[8,2,1,16,1,2048]{5,3,4,2,1,0:T(8,128)}), f32[1,2,1,16,1,2048]{5,3,4,2,1,0:T(8,128)}) %reduce-scatter.9.cloned.1.call-update) | async-done | bytes 262160 | tf_op jit(solution)/shard_map/reduce_scatter | solution.py:39
  364.3 233.1 %all-reduce.6.cloned.1.call-done = f32[160,16,16]{0,2,1:T(8,128)} async-done(((f32[160,16,16]{0,2,1:T(8,128)}), f32[160,16,16]{0,2,1:T(8,128)}) %all-reduce.6.cloned.1.call-update) | async-done | bytes 163856 | tf_op jit(solution)/shard_map/psum | solution.py:164
  603.6 16.7 %reduce-scatter.15.cloned.1.call-done = f32[1,1,1,64,1,512]{5,3,2,1,0,4:T(8,128)} async-done(((f32[1,2,1,64,1,512]{5,3,2,1,0,4:T(8,128)}), f32[1,1,1,64,1,512]{5,3,2,1,0,4:T(8,128)}) %reduce-scatter.15.cloned.1.call-update) | async-done | bytes 131088 | tf_op jit(solution)/shard_map/reduce_scatter | solution.py:40
  620.3 23.2 %reduce-scatter.11.cloned.1.call-done = f32[1,1,1,16,1,2048]{5,3,4,2,1,0:T(8,128)} async-done(((f32[1,2,1,16,1,2048]{5,3,4,2,1,0:T(8,128)}), f32[1,1,1,16,1,2048]{5,3,4,2,1,0:T(8,128)}) %reduce-scatter.11.cloned.1.call-update) | async-done | bytes 131088 | tf_op jit(solution)/shard_map/reduce_scatter | solution.py:40
  (84 shorter events, 57.2 us)
Async XLA Ops:
  7.2 73.8 %copy-start = (bf16[256,512]{1,0:T(8,128)(2,1)S(1)}, bf16[256,512]{1,0:T(8,128)(2,1)}, u32[]{:S(2)}) copy-start(bf16[256,512]{1,0:T(8,128)(2,1)} %param.6) | copy-start | bytes 786436
  7.2 48.8 %all-gather.13.cloned.1.call-start = ((), (), s32[]{:S(2)}) async-start(), calls=%async_computation.19 | async-start | bytes 1179648 | tf_op jit(solution)/shard_map/all_gather | solution.py:49
  13.6 67.3 %all-gather.9.cloned.1.call-start = ((), (), s32[]{:S(2)}) async-start(), calls=%async_computation.12 | async-start | bytes 3145728 | tf_op jit(solution)/shard_map/all_gather | solution.py:50
  56.0 64.5 %all-gather.15.cloned.1.call-start = ((), (), s32[]{:S(2)}) async-start(), calls=%async_computation.20 | async-start | bytes 1179648 | tf_op jit(solution)/shard_map/all_gather | solution.py:49
  62.3 3.5 copy-start.9
  66.9 17.5 %all-to-all-start.4 = ((bf16[256,4,4,32]{0,3,1,2:T(8,128)(2,1)}), bf16[256,4,4,32]{0,3,1,2:T(8,128)(2,1)S(1)}, u32[]{:S(2)}, u32[]{:S(2)}) async-start(bf16[256,4,4,32]{0,3,1,2:T(8,128)(2,1)} %copy.90), calls=%async_computation.4 | async-start | bytes 524288 | tf_op jit(solution)/shard_map/all_to_all | solution.py:27
  84.4 37.0 %all-to-all-start = ((bf16[256,4,4,128]{0,3,1,2:T(8,128)(2,1)}), bf16[256,4,4,128]{0,3,1,2:T(8,128)(2,1)S(1)}, u32[]{:S(2)}, u32[]{:S(2)}) async-start(bf16[256,4,4,128]{0,3,1,2:T(8,128)(2,1)} %copy.81), calls=%async_computation | async-start | bytes 2097152 | tf_op jit(solution)/shard_map/all_to_all | solution.py:27
  87.9 57.4 %all-gather.11.cloned.1.call-start = ((), (), s32[]{:S(2)}) async-start(), calls=%async_computation.13 | async-start | bytes 3145728 | tf_op jit(solution)/shard_map/all_gather | solution.py:50
  121.3 14.4 %all-to-all-start.5 = ((bf16[256,4,4,32]{0,3,2,1:T(8,128)(2,1)}), bf16[256,4,4,32]{0,3,2,1:T(8,128)(2,1)S(1)}, u32[]{:S(2)}, u32[]{:S(2)}) async-start(bf16[256,4,4,32]{0,3,2,1:T(8,128)(2,1)} %copy.91), calls=%async_computation.5 | async-start | bytes 524288 | tf_op jit(solution)/shard_map/all_to_all | solution.py:28
  127.8 12.2 %copy-start.11 = (bf16[128,16,16]{0,2,1:T(8,128)(2,1)S(1)}, bf16[128,16,16]{0,2,1:T(8,128)(2,1)}, u32[]{:S(2)}) copy-start(bf16[128,16,16]{0,2,1:T(8,128)(2,1)} %param.8) | copy-start | bytes 196612
  135.7 30.0 %all-to-all-start.1 = ((bf16[256,4,4,128]{0,3,2,1:T(8,128)(2,1)}), bf16[256,4,4,128]{0,3,2,1:T(8,128)(2,1)}, u32[]{:S(2)}, u32[]{:S(2)}) async-start(bf16[256,4,4,128]{0,3,2,1:T(8,128)(2,1)} %copy.82), calls=%async_computation.1 | async-start | bytes 2097152 | tf_op jit(solution)/shard_map/all_to_all | solution.py:28
  165.7 5.5 copy-start.7
  187.3 7.6 %copy-start.8 = (bf16[256,16,128]{0,1,2:T(8,128)(2,1)S(1)}, bf16[256,16,128]{0,1,2:T(8,128)(2,1)}, u32[]{:S(2)}) copy-start(bf16[256,16,128]{0,1,2:T(8,128)(2,1)} %get-tuple-element.21) | copy-start | bytes 3145732
  188.4 26.3 %all-to-all-start.7 = ((bf16[256,4,4,128]{0,3,2,1:T(8,128)(2,1)}), bf16[256,4,4,128]{0,3,2,1:T(8,128)(2,1)S(1)}, u32[]{:S(2)}, u32[]{:S(2)}) async-start(bf16[256,4,4,128]{0,3,2,1:T(8,128)(2,1)} %copy.96), calls=%async_computation.7 | async-start | bytes 2097152 | tf_op jit(solution)/shard_map/all_to_all | solution.py:28
  194.9 76.8 %all-reduce.8.cloned.1.call-start = ((), (), s32[]{:S(2)}) async-start(), calls=%async_computation.21 | async-start | bytes 16777216
  217.4 99.6 %reduce-scatter.13.cloned.1.call-start = ((), (), s32[]{:S(2)}) async-start(), calls=%async_computation.17 | async-start | bytes 2359296 | tf_op jit(solution)/shard_map/reduce_scatter | solution.py:39
  275.6 87.7 %reduce-scatter.9.cloned.1.call-start = ((), (), s32[]{:S(2)}) async-start(), calls=%async_computation.14 | async-start | bytes 2359296 | tf_op jit(solution)/shard_map/reduce_scatter | solution.py:39
  283.1 17.4 %copy-start.3 = (bf16[256,16,128]{0,1,2:T(8,128)(2,1)S(1)}, bf16[256,16,128]{0,1,2:T(8,128)(2,1)}, u32[]{:S(2)}) copy-start(bf16[256,16,128]{0,1,2:T(8,128)(2,1)} %copy-done.2) | copy-start | bytes 3145732
  293.1 14.8 %all-to-all-start.3 = ((bf16[256,4,4,32]{0,3,2,1:T(8,128)(2,1)}), bf16[256,4,4,32]{0,3,2,1:T(8,128)(2,1)S(1)}, u32[]{:S(2)}, u32[]{:S(2)}) async-start(bf16[256,4,4,32]{0,3,2,1:T(8,128)(2,1)} %copy.88), calls=%async_computation.3 | async-start | bytes 524288 | tf_op jit(solution)/shard_map/all_to_all | solution.py:28
  299.6 297.9 %all-reduce.6.cloned.1.call-start = ((), (), s32[]{:S(2)}) async-start(), calls=%async_computation.16 | async-start | bytes 524288 | tf_op jit(solution)/shard_map/psum | solution.py:164
  300.4 7.5 %copy-start.10 = (bf16[256,512]{0,1:T(8,128)(2,1)S(1)}, bf16[256,512]{0,1:T(8,128)(2,1)}, u32[]{:S(2)}) copy-start(bf16[256,512]{0,1:T(8,128)(2,1)} %copy.99) | copy-start | bytes 786436
  302.9 297.7 %copy-start.5 = (bf16[256,4,4,128]{0,3,2,1:T(8,128)(2,1)S(1)}, bf16[256,4,4,128]{0,3,2,1:T(8,128)(2,1)}, u32[]{:S(2)}) copy-start(bf16[256,4,4,128]{0,3,2,1:T(8,128)(2,1)} %copy-done.4) | copy-start | bytes 3145732
  309.3 311.0 %reduce-scatter.15.cloned.1.call-start = ((), (), s32[]{:S(2)}) async-start(), calls=%async_computation.18 | async-start | bytes 393216 | tf_op jit(solution)/shard_map/reduce_scatter | solution.py:40
  317.0 326.5 %reduce-scatter.11.cloned.1.call-start = ((), (), s32[]{:S(2)}) async-start(), calls=%async_computation.15 | async-start | bytes 393216 | tf_op jit(solution)/shard_map/reduce_scatter | solution.py:40
  (4 other events, 6.4 us)
Sparse Core Ops, SparseCore 0:
  13.7 42.2 all-gather.12
  58.1 22.8 all-gather.8
  83.0 37.5 all-gather.14
  122.5 22.7 all-gather.10
  217.5 54.1 all-reduce.7
  275.7 41.1 reduce-scatter.12
  319.8 43.4 reduce-scatter.8
  366.7 230.6 all-reduce.5
  601.0 19.2 reduce-scatter.14
  623.5 19.9 reduce-scatter.10
where the time goes:
time: 652 us; the launch traced here: 650 us
  waiting for transfers between devices  509 us (78%)
  blocking collectives  35.8 us (5%)
  local copies, waits for them, and re-layouts  33.3 us (5%)
  starting transfers between devices  31.5 us (5%)
  matrix products  23.7 us (4%)
  between operations  14.3 us (2%)
    psum x1, waiting for transfers between devices, on_device(): rights = lax.psum(rights, DP_AXES)  233 us
    all_gather x2, waiting for transfers between devices, dp_all_gather(): x = lax.all_gather(x, 'z', axis=row_axis, tiled=True)  75 us
    reduce_scatter x2, waiting for transfers between devices, dp_reduce_scatter(): x = lax.psum_scatter(x, 'z', scatter_dimension=row_axis, tiled=True)  53.9 us
    unnamed x11, waiting for transfers between devices  53.1 us
    all_to_all x4, waiting for transfers between devices, exchange(): shaped = lax.all_to_all(shaped, 'yhi', 1, 1, tiled=True)  40.3 us
    reduce_scatter x2, waiting for transfers between devices, dp_reduce_scatter(): x = lax.psum_scatter(x, 'ylo', scatter_dimension=row_axis + 1, tiled=True)  39.8 us
    all_to_all x2, blocking collectives, exchange(): shaped = lax.all_to_all(shaped, 'x', 2, 2, tiled=True)  24.2 us
    all_to_all x4, starting transfers between devices, exchange(): shaped = lax.all_to_all(shaped, 'yhi', 1, 1, tiled=True)  23.7 us
  transfers between devices with their start and end apart: 16, of which 14 were waited for; matrix products, arithmetic and copies ran while one was open for 7% of the time, Pallas kernels for 0%

commit v1 on v0

--- a/solution.py
+++ b/solution.py
@@ -161,7 +161,7 @@
         0,
     ).transpose(1, 0, 2)
     rights = jnp.concatenate([right_up_term, right_down_term], axis=0)
-    rights = lax.psum(rights, DP_AXES)
+    rights = lax.psum(lax.psum(rights, ("ylo", "core")), "z")
     grad_up_right = rights[:group_up]
     grad_down_right = rights[group_up:]
     return (layer_out, grad_tokens, grad_up_left, grad_up_right, grad_down_left, grad_down_right)

time: 652 us -> 549 us (0.84)
  waiting for transfers between devices: 509 us -> 411 us
    psum x1 -> x2, waiting for transfers between devices: 233 us -> 121 us  [on_device(): rights = lax.psum(lax.psum(rights, ('ylo', 'core')), 'z')]
    reduce_scatter x2, waiting for transfers between devices: 53.9 us -> 90.7 us  [dp_reduce_scatter(): x = lax.psum_scatter(x, 'z', scatter_dimension=row_axis, tiled=True)]
    unnamed x11 -> x12, waiting for transfers between devices: 53.1 us -> 29 us
  transfers between devices with their start and end apart: 16 -> 17, of which waited for: 14 -> 15; matrix products, arithmetic and copies ran while one was open for 7% -> 8% of each run, Pallas kernels for 0% -> 0%
where the time goes in v1:
time: 549 us; the launch traced here: 548 us
  waiting for transfers between devices  411 us (75%)
  blocking collectives  34.7 us (6%)
  local copies, waits for them, and re-layouts  33.3 us (6%)
  starting transfers between devices  29.1 us (5%)
  matrix products  24 us (4%)
  between operations  14.1 us (3%)
    psum x2, waiting for transfers between devices, on_device(): rights = lax.psum(lax.psum(rights, ('ylo', 'core')), 'z')  121 us
    reduce_scatter x2, waiting for transfers between devices, dp_reduce_scatter(): x = lax.psum_scatter(x, 'z', scatter_dimension=row_axis, tiled=True)  90.7 us
    all_gather x2, waiting for transfers between devices, dp_all_gather(): x = lax.all_gather(x, 'z', axis=row_axis, tiled=True)  75 us
    reduce_scatter x2, waiting for transfers between devices, dp_reduce_scatter(): x = lax.psum_scatter(x, 'ylo', scatter_dimension=row_axis + 1, tiled=True)  42.9 us
    all_to_all x4, waiting for transfers between devices, exchange(): shaped = lax.all_to_all(shaped, 'yhi', 1, 1, tiled=True)  38.2 us
    unnamed x12, waiting for transfers between devices  29 us
    all_to_all x2, blocking collectives, exchange(): shaped = lax.all_to_all(shaped, 'x', 2, 2, tiled=True)  23.1 us
    all_to_all x4, starting transfers between devices, exchange(): shaped = lax.all_to_all(shaped, 'yhi', 1, 1, tiled=True)  21.3 us
  transfers between devices with their start and end apart: 17, of which 15 were waited for; matrix products, arithmetic and copies ran while one was open for 8% of the time, Pallas kernels for 0%

profile of v1, /device:TPU:1, one launch (start us, length us, event | category | flops | bytes accessed | tf_op | source)
XLA Modules:
  0.0 548.0 jit_solution(1807875059190053653)
XLA Ops:
  7.2 6.3 %all-gather = bf16[2,16,2048]{2,1,0:T(8,128)(2,1)} all-gather(bf16[1,16,2048]{2,1,0:T(8,128)(2,1)} %param.7), channel_id=2, replica_groups=mesh['z'=8,'ylo'=2,'core'=2,'yhi'=4,'x'=4] {'ylo'}, dimensions={0}, use_global_device_ids=true | all-gather | bytes 196608 | tf_op jit(solution)/shard_map/all_gather | solution.py:48
  13.6 42.4 %all-gather.13.cloned.1.call-done = bf16[16,16,2048]{2,1,0:T(8,128)(2,1)} async-done(((bf16[2,16,2048]{2,1,0:T(8,128)(2,1)}), bf16[16,16,2048]{2,1,0:T(8,128)(2,1)}) %all-gather.13.cloned.1.call-update) | async-done | bytes 1048592 | tf_op jit(solution)/shard_map/all_gather | solution.py:49
  56.1 5.3 all-gather.2
  70.8 10.1 %all-gather.9.cloned.1.call-done = bf16[1,8,2,2,16,2048]{5,4,3,2,1,0:T(8,128)(2,1)} async-done(((bf16[1,8,2,1,16,2048]{5,4,3,2,1,0:T(8,128)(2,1)}), bf16[1,8,2,2,16,2048]{5,4,3,2,1,0:T(8,128)(2,1)}) %all-gather.9.cloned.1.call-update) | async-done | bytes 2097168 | tf_op jit(solution)/shard_map/all_gather | solution.py:50
  87.9 32.6 %all-gather.15.cloned.1.call-done = bf16[16,64,512]{2,1,0:T(8,128)(2,1)} async-done(((bf16[2,64,512]{2,1,0:T(8,128)(2,1)}), bf16[16,64,512]{2,1,0:T(8,128)(2,1)}) %all-gather.15.cloned.1.call-update) | async-done | bytes 1048592 | tf_op jit(solution)/shard_map/all_gather | solution.py:49
  121.3 6.5 %all-to-all-start.5 = ((bf16[256,4,4,32]{0,3,2,1:T(8,128)(2,1)}), bf16[256,4,4,32]{0,3,2,1:T(8,128)(2,1)S(1)}, u32[]{:S(2)}, u32[]{:S(2)}) async-start(bf16[256,4,4,32]{0,3,2,1:T(8,128)(2,1)} %copy.91), calls=%async_computation.5 | async-start | bytes 524288 | tf_op jit(solution)/shard_map/all_to_all | solution.py:28
  128.8 6.9 %all-to-all-done.5 = bf16[256,4,4,32]{0,3,2,1:T(8,128)(2,1)S(1)} async-done(((bf16[256,4,4,32]{0,3,2,1:T(8,128)(2,1)}), bf16[256,4,4,32]{0,3,2,1:T(8,128)(2,1)S(1)}, u32[]{:S(2)}, u32[]{:S(2)}) %all-to-all-start.5) | async-done | bytes 262176 | tf_op jit(solution)/shard_map/all_to_all | solution.py:28
  135.7 4.2 all-to-all-start.1
  141.1 4.2 all-gather.11.cloned.1.call-done
  147.6 18.1 %all-to-all-done.1 = bf16[256,4,4,128]{0,3,2,1:T(8,128)(2,1)} async-done(((bf16[256,4,4,128]{0,3,2,1:T(8,128)(2,1)}), bf16[256,4,4,128]{0,3,2,1:T(8,128)(2,1)}, u32[]{:S(2)}, u32[]{:S(2)}) %all-to-all-start.1) | async-done | bytes 1048608 | tf_op jit(solution)/shard_map/all_to_all | solution.py:28
  165.7 4.5 fusion.7
  172.2 15.0 %all_to_all.40 = bf16[256,4,4,128]{0,3,1,2:T(8,128)(2,1)S(1)} all-to-all(bf16[256,4,4,128]{0,3,1,2:T(8,128)(2,1)S(1)} %copy.95), channel_id=1, replica_groups=mesh['z'=8,'ylo'=2,'core'=2,'yhi'=4,'x'=4] {'x'}, dimensions={2} | all-to-all | bytes 2097152 | tf_op jit(solution)/shard_map/all_to_all | solution.py:27
  188.3 6.5 %all-to-all-start.7 = ((bf16[256,4,4,128]{0,3,2,1:T(8,128)(2,1)}), bf16[256,4,4,128]{0,3,2,1:T(8,128)(2,1)S(1)}, u32[]{:S(2)}, u32[]{:S(2)}) async-start(bf16[256,4,4,128]{0,3,2,1:T(8,128)(2,1)} %copy.96), calls=%async_computation.7 | async-start | bytes 2097152 | tf_op jit(solution)/shard_map/all_to_all | solution.py:28
  199.0 5.4 copy.103
  204.5 10.1 %all-to-all-done.7 = bf16[256,4,4,128]{0,3,2,1:T(8,128)(2,1)S(1)} async-done(((bf16[256,4,4,128]{0,3,2,1:T(8,128)(2,1)}), bf16[256,4,4,128]{0,3,2,1:T(8,128)(2,1)S(1)}, u32[]{:S(2)}, u32[]{:S(2)}) %all-to-all-start.7) | async-done | bytes 1048608 | tf_op jit(solution)/shard_map/all_to_all | solution.py:28
  221.0 8.0 %all_to_all.41 = bf16[256,4,4,32]{0,3,1,2:T(8,128)(2,1)S(1)} all-to-all(bf16[256,4,4,32]{0,3,1,2:T(8,128)(2,1)S(1)} %copy.87), channel_id=1, replica_groups=mesh['z'=8,'ylo'=2,'core'=2,'yhi'=4,'x'=4] {'x'}, dimensions={2} | all-to-all | bytes 524288 | tf_op jit(solution)/shard_map/all_to_all | solution.py:27
  229.8 4.1 all-to-all-start.3
  243.1 28.8 %all-reduce.11.cloned.1.call-done = (f32[8,2,2,16,1,2048]{5,3,4,2,1,0:T(8,128)}, f32[8,2,2,64,1,512]{5,3,2,1,0,4:T(8,128)}) async-done(((f32[8,2,2,16,1,2048]{5,3,4,2,1,0:T(8,128)}, f32[8,2,2,64,1,512]{5,3,2,1,0,4:T(8,128)}), (f32[8,2,2,16,1,2048]{5,3,4,2,1,0:T(8,128)}, f32[8,2,2,64,1,512]{5,3,2,1,0,4:T(8,128)})) %all-reduce.11.cloned.1.call-update) | async-done | bytes 8388624
  279.9 42.3 %all-reduce.7.cloned.1.call-done = f32[160,16,16]{0,2,1:T(8,128)} async-done(((f32[160,16,16]{0,2,1:T(8,128)}), f32[160,16,16]{0,2,1:T(8,128)}) %all-reduce.7.cloned.1.call-update) | async-done | bytes 163856 | tf_op jit(solution)/shard_map/psum | solution.py:164
  322.2 44.2 %reduce-scatter.13.cloned.1.call-done = f32[1,2,1,64,1,512]{5,3,2,1,0,4:T(8,128)} async-done(((f32[8,2,1,64,1,512]{5,3,2,1,0,4:T(8,128)}), f32[1,2,1,64,1,512]{5,3,2,1,0,4:T(8,128)}) %reduce-scatter.13.cloned.1.call-update) | async-done | bytes 262160 | tf_op jit(solution)/shard_map/reduce_scatter | solution.py:39
  366.5 46.5 %reduce-scatter.9.cloned.1.call-done = f32[1,2,1,16,1,2048]{5,3,4,2,1,0:T(8,128)} async-done(((f32[8,2,1,16,1,2048]{5,3,4,2,1,0:T(8,128)}), f32[1,2,1,16,1,2048]{5,3,4,2,1,0:T(8,128)}) %reduce-scatter.9.cloned.1.call-update) | async-done | bytes 262160 | tf_op jit(solution)/shard_map/reduce_scatter | solution.py:39
  414.1 78.3 %all-reduce.9.cloned.1.call-done = f32[160,16,16]{0,2,1:T(8,128)} async-done(((f32[160,16,16]{0,2,1:T(8,128)}), f32[160,16,16]{0,2,1:T(8,128)}) %all-reduce.9.cloned.1.call-update) | async-done | bytes 163856 | tf_op jit(solution)/shard_map/psum | solution.py:164
  498.6 19.3 %reduce-scatter.15.cloned.1.call-done = f32[1,1,1,64,1,512]{5,3,2,1,0,4:T(8,128)} async-done(((f32[1,2,1,64,1,512]{5,3,2,1,0,4:T(8,128)}), f32[1,1,1,64,1,512]{5,3,2,1,0,4:T(8,128)}) %reduce-scatter.15.cloned.1.call-update) | async-done | bytes 131088 | tf_op jit(solution)/shard_map/reduce_scatter | solution.py:40
  517.9 23.6 %reduce-scatter.11.cloned.1.call-done = f32[1,1,1,16,1,2048]{5,3,4,2,1,0:T(8,128)} async-done(((f32[1,2,1,16,1,2048]{5,3,4,2,1,0:T(8,128)}), f32[1,1,1,16,1,2048]{5,3,4,2,1,0:T(8,128)}) %reduce-scatter.11.cloned.1.call-update) | async-done | bytes 131088 | tf_op jit(solution)/shard_map/reduce_scatter | solution.py:40
  (87 shorter events, 60.6 us)
Async XLA Ops:
  7.2 73.8 %copy-start = (bf16[256,512]{1,0:T(8,128)(2,1)S(1)}, bf16[256,512]{1,0:T(8,128)(2,1)}, u32[]{:S(2)}) copy-start(bf16[256,512]{1,0:T(8,128)(2,1)} %param.6) | copy-start | bytes 786436
  7.2 48.8 %all-gather.13.cloned.1.call-start = ((), (), s32[]{:S(2)}) async-start(), calls=%async_computation.20 | async-start | bytes 1179648 | tf_op jit(solution)/shard_map/all_gather | solution.py:49
  13.6 67.3 %all-gather.9.cloned.1.call-start = ((), (), s32[]{:S(2)}) async-start(), calls=%async_computation.12 | async-start | bytes 3145728 | tf_op jit(solution)/shard_map/all_gather | solution.py:50
  56.0 64.5 %all-gather.15.cloned.1.call-start = ((), (), s32[]{:S(2)}) async-start(), calls=%async_computation.21 | async-start | bytes 1179648 | tf_op jit(solution)/shard_map/all_gather | solution.py:49
  66.9 17.5 %all-to-all-start.4 = ((bf16[256,4,4,32]{0,3,1,2:T(8,128)(2,1)}), bf16[256,4,4,32]{0,3,1,2:T(8,128)(2,1)S(1)}, u32[]{:S(2)}, u32[]{:S(2)}) async-start(bf16[256,4,4,32]{0,3,1,2:T(8,128)(2,1)} %copy.90), calls=%async_computation.4 | async-start | bytes 524288 | tf_op jit(solution)/shard_map/all_to_all | solution.py:27
  84.4 36.9 %all-to-all-start = ((bf16[256,4,4,128]{0,3,1,2:T(8,128)(2,1)}), bf16[256,4,4,128]{0,3,1,2:T(8,128)(2,1)S(1)}, u32[]{:S(2)}, u32[]{:S(2)}) async-start(bf16[256,4,4,128]{0,3,1,2:T(8,128)(2,1)} %copy.81), calls=%async_computation | async-start | bytes 2097152 | tf_op jit(solution)/shard_map/all_to_all | solution.py:27
  87.9 57.4 %all-gather.11.cloned.1.call-start = ((), (), s32[]{:S(2)}) async-start(), calls=%async_computation.13 | async-start | bytes 3145728 | tf_op jit(solution)/shard_map/all_gather | solution.py:50
  121.3 14.4 %all-to-all-start.5 = ((bf16[256,4,4,32]{0,3,2,1:T(8,128)(2,1)}), bf16[256,4,4,32]{0,3,2,1:T(8,128)(2,1)S(1)}, u32[]{:S(2)}, u32[]{:S(2)}) async-start(bf16[256,4,4,32]{0,3,2,1:T(8,128)(2,1)} %copy.91), calls=%async_computation.5 | async-start | bytes 524288 | tf_op jit(solution)/shard_map/all_to_all | solution.py:28
  127.8 12.2 %copy-start.11 = (bf16[128,16,16]{0,2,1:T(8,128)(2,1)S(1)}, bf16[128,16,16]{0,2,1:T(8,128)(2,1)}, u32[]{:S(2)}) copy-start(bf16[128,16,16]{0,2,1:T(8,128)(2,1)} %param.8) | copy-start | bytes 196612
  135.7 30.0 %all-to-all-start.1 = ((bf16[256,4,4,128]{0,3,2,1:T(8,128)(2,1)}), bf16[256,4,4,128]{0,3,2,1:T(8,128)(2,1)}, u32[]{:S(2)}, u32[]{:S(2)}) async-start(bf16[256,4,4,128]{0,3,2,1:T(8,128)(2,1)} %copy.82), calls=%async_computation.1 | async-start | bytes 2097152 | tf_op jit(solution)/shard_map/all_to_all | solution.py:28
  165.7 5.5 copy-start.7
  187.2 7.6 %copy-start.8 = (bf16[256,16,128]{0,1,2:T(8,128)(2,1)S(1)}, bf16[256,16,128]{0,1,2:T(8,128)(2,1)}, u32[]{:S(2)}) copy-start(bf16[256,16,128]{0,1,2:T(8,128)(2,1)} %get-tuple-element.21) | copy-start | bytes 3145732
  188.3 26.3 %all-to-all-start.7 = ((bf16[256,4,4,128]{0,3,2,1:T(8,128)(2,1)}), bf16[256,4,4,128]{0,3,2,1:T(8,128)(2,1)S(1)}, u32[]{:S(2)}, u32[]{:S(2)}) async-start(bf16[256,4,4,128]{0,3,2,1:T(8,128)(2,1)} %copy.96), calls=%async_computation.7 | async-start | bytes 2097152 | tf_op jit(solution)/shard_map/all_to_all | solution.py:28
  194.8 77.1 %all-reduce.11.cloned.1.call-start = ((), (), s32[]{:S(2)}) async-start(), calls=%async_computation.22 | async-start | bytes 16777216
  220.8 15.1 %copy-start.3 = (bf16[256,16,128]{0,1,2:T(8,128)(2,1)S(1)}, bf16[256,16,128]{0,1,2:T(8,128)(2,1)}, u32[]{:S(2)}) copy-start(bf16[256,16,128]{0,1,2:T(8,128)(2,1)} %copy-done.2) | copy-start | bytes 3145732
  229.8 12.0 %all-to-all-start.3 = ((bf16[256,4,4,32]{0,3,2,1:T(8,128)(2,1)}), bf16[256,4,4,32]{0,3,2,1:T(8,128)(2,1)S(1)}, u32[]{:S(2)}, u32[]{:S(2)}) async-start(bf16[256,4,4,32]{0,3,2,1:T(8,128)(2,1)} %copy.88), calls=%async_computation.3 | async-start | bytes 524288 | tf_op jit(solution)/shard_map/all_to_all | solution.py:28
  233.8 88.3 %all-reduce.7.cloned.1.call-start = ((), (), s32[]{:S(2)}) async-start(), calls=%async_computation.16 | async-start | bytes 524288 | tf_op jit(solution)/shard_map/psum | solution.py:164
  236.0 5.8 %copy-start.10 = (bf16[256,512]{0,1:T(8,128)(2,1)S(1)}, bf16[256,512]{0,1:T(8,128)(2,1)}, u32[]{:S(2)}) copy-start(bf16[256,512]{0,1:T(8,128)(2,1)} %copy.99) | copy-start | bytes 786436
  243.1 123.3 %reduce-scatter.13.cloned.1.call-start = ((), (), s32[]{:S(2)}) async-start(), calls=%async_computation.18 | async-start | bytes 2359296 | tf_op jit(solution)/shard_map/reduce_scatter | solution.py:39
  275.9 137.2 %reduce-scatter.9.cloned.1.call-start = ((), (), s32[]{:S(2)}) async-start(), calls=%async_computation.14 | async-start | bytes 2359296 | tf_op jit(solution)/shard_map/reduce_scatter | solution.py:39
  279.8 215.7 %copy-start.5 = (bf16[256,4,4,128]{0,3,2,1:T(8,128)(2,1)S(1)}, bf16[256,4,4,128]{0,3,2,1:T(8,128)(2,1)}, u32[]{:S(2)}) copy-start(bf16[256,4,4,128]{0,3,2,1:T(8,128)(2,1)} %copy-done.4) | copy-start | bytes 3145732
  279.8 212.6 %all-reduce.9.cloned.1.call-start = ((), (), s32[]{:S(2)}) async-start(), calls=%async_computation.17 | async-start | bytes 524288 | tf_op jit(solution)/shard_map/psum | solution.py:164
  322.2 195.7 %reduce-scatter.15.cloned.1.call-start = ((), (), s32[]{:S(2)}) async-start(), calls=%async_computation.19 | async-start | bytes 393216 | tf_op jit(solution)/shard_map/reduce_scatter | solution.py:40
  366.5 175.0 %reduce-scatter.11.cloned.1.call-start = ((), (), s32[]{:S(2)}) async-start(), calls=%async_computation.15 | async-start | bytes 393216 | tf_op jit(solution)/shard_map/reduce_scatter | solution.py:40
  (5 other events, 9.8 us)
Sparse Core Ops, SparseCore 0:
  13.7 42.2 all-gather.12
  58.1 22.8 all-gather.8
  83.0 37.5 all-gather.14
  122.5 22.7 all-gather.10
  217.4 54.4 all-reduce.10
  275.3 46.7 all-reduce.6
  325.2 41.1 reduce-scatter.12
  369.5 43.4 reduce-scatter.8
  415.5 76.8 all-reduce.8
  495.6 22.2 reduce-scatter.14
  521.4 19.9 reduce-scatter.10
